TPU v7x, 128 devices: a whole 4x4x4 slice. The times are simulated.
128 devices in a mesh: seq: 16 (over z, x_hi, core), head: 8 (over y, x_lo).
Axes of the slice: x: 4 (x_hi: 2, x_lo: 2; x = x_hi * 2 + x_lo), y: 4, z: 4, core: 2. Of those that a mesh axis runs over, the one named last changes fastest.
Arguments:
- queries: bfloat16 [16384, 4096], P('seq', 'head'), may hold values from -6 to 6
- key_rows: bfloat16 [16384, 4096], P('seq', 'head'), may hold values from -6 to 6
- value_rows: bfloat16 [16384, 4096], P('seq', 'head'), may hold values from -6 to 6
- out_weight: bfloat16 [4096, 4096], P('head'), may hold values from -0.375 to 0.375
- cotangent: bfloat16 [16384, 4096], P('seq', 'head'), may hold values from -1.5 to 1.5
- pattern: int32 [128, 7], P('seq'), may hold values 0 or 1
Outputs:
- output: bfloat16 [16384, 4096], P('seq', 'head')
- grad_query: bfloat16 [16384, 4096], P('seq', 'head')
- grad_keys: bfloat16 [16384, 4096], P('seq', 'head')
- grad_values: bfloat16 [16384, 4096], P('seq', 'head')
- grad_weight: float32 [4096, 4096], P('seq', 'head')
All inputs are finite; a program needn't handle non-finite values. No bound on the sum of `pattern` on one device may be relied on, other than what follows from the above.
Results may differ from a plain program's by a relative error of at most 0.0076.
Values may be sent and summed in bfloat16 or wider, within the bound.
No kernel may reach another device: no remote copies, remote signals or barrier semaphores. Data moves between devices by JAX's collectives and lax.ppermute only.
A program may use at most 256 MiB of HBM per device.

v0:
```python
import math
import jax
import jax.numpy as jnp
from jax import lax
from jax.sharding import PartitionSpec as P

DH = 128
BLK = 128
LOG_TWO = math.log(2.0)


def swapped(value, axis, bit):
    mask = 2**bit
    pairs = [(source, source ^ mask) for source in range(lax.axis_size(axis))]
    return lax.ppermute(value, axis, pairs)


def pair_mean(tensor):
    shape_in = tensor.shape
    paired = tensor.reshape(shape_in[:-2] + (shape_in[-2] // 2, 2, shape_in[-1]))
    return jnp.sum(paired, axis=-2) * 0.5


def spread_rows(grads, factor):
    shape_in = grads.shape
    wide = jnp.broadcast_to(grads[..., :, None, :], shape_in[:-1] + (factor, shape_in[-1])) * (
        1.0 / factor
    )
    return wide.reshape(shape_in[:-2] + (shape_in[-2] * factor, shape_in[-1]))


def head_ring_gather(value, relative=False):
    count = lax.axis_size("head")
    rings = count // 2
    width = value.shape[-1]
    where_head = lax.axis_index("head")
    ring_pos = where_head // 2
    partner = lax.ppermute(value, "head", [(src, src ^ 1) for src in range(count)])
    low_first = where_head % 2 == 0
    if relative:
        pair_block = jnp.concatenate([value, partner], axis=-1)
    else:
        pair_block = jnp.concatenate(
            [jnp.where(low_first, value, partner), jnp.where(low_first, partner, value)], axis=-1
        )
    upward = [(src, (src // 2 + 1) % rings * 2 + src % 2) for src in range(count)]
    downward = [(src, (src // 2 - 1) % rings * 2 + src % 2) for src in range(count)]
    from_below = lax.ppermute(pair_block, "head", upward)
    from_above = lax.ppermute(pair_block, "head", downward)
    blocks = [pair_block, from_above]
    if rings == 4:
        far = jnp.concatenate(
            [
                lax.ppermute(from_below[..., :width], "head", upward),
                lax.ppermute(from_above[..., width:], "head", downward),
            ],
            axis=-1,
        )
        blocks = [pair_block, from_above, far, from_below]
    if relative:
        return blocks
    stacked = jnp.stack(blocks)
    order = (jnp.arange(rings) - ring_pos) % rings
    placed = stacked[order]
    return jnp.moveaxis(placed, 0, -2).reshape(value.shape[:-1] + (rings * 2 * width,))


def weight_columns(out_weight):
    count = lax.axis_size("head")
    seq_count = lax.axis_size("seq")
    where_head = lax.axis_index("head")
    core = lax.axis_index("seq") % 2
    rows, cols = out_weight.shape
    width = cols // count
    own = lax.dynamic_slice_in_dim(out_weight, where_head * width, width, axis=1)
    fetched = []
    for step in range(count // 2):
        shift_low, shift_high = (2 * step + 1, 2 * step + 2)
        pairs = []
        for seq_idx in range(seq_count):
            shift = shift_low if seq_idx % 2 == 0 else shift_high
            if shift % count == 0:
                continue
            for src in range(count):
                pairs.append((seq_idx * count + src, seq_idx * count + (src + shift) % count))
        shift = jnp.where(core == 0, shift_low, shift_high)
        outgoing = lax.dynamic_slice_in_dim(
            out_weight, (where_head + shift) % count * width, width, axis=1
        )
        fetched.append(lax.ppermute(outgoing, ("seq", "head"), pairs))
    mine = jnp.stack(fetched)
    theirs = lax.ppermute(mine, "seq", [(src, src ^ 1) for src in range(seq_count)])
    odd = jnp.where(core == 0, mine, theirs)
    even = jnp.where(core == 0, theirs, mine)
    by_shift = [own]
    for shift in range(1, count):
        by_shift.append(odd[(shift - 1) // 2] if shift % 2 else even[shift // 2 - 1])
    low_first = where_head % 2 == 0
    ring_blocks = []
    for dist in range(count // 2):
        ring_blocks.append(
            jnp.concatenate(
                [
                    by_shift[-2 * dist % count],
                    jnp.where(
                        low_first,
                        by_shift[(-1 - 2 * dist) % count],
                        by_shift[(1 - 2 * dist) % count],
                    ),
                ],
                axis=0,
            )
        )
    return ring_blocks


def body(queries, key_rows, value_rows, out_weight, cotangent, pattern):
    row_count, features = queries.shape
    blocks = row_count // BLK
    local_levels = blocks.bit_length() - 1
    seq_count = lax.axis_size("seq")
    cross_levels = seq_count.bit_length() - 1
    level_count = local_levels + cross_levels
    head_count = features // DH
    keys_all = (1 + level_count) * BLK
    score_scale = DH ** (-0.5)
    where_seq = lax.axis_index("seq")
    stacked = jnp.stack([key_rows, value_rows])
    coarse_base = (
        stacked.reshape(2, BLK, row_count // BLK, features).astype(jnp.float32).mean(axis=2)
    )
    siblings = []
    current = coarse_base
    for level_idx in range(cross_levels):
        received = swapped(current, "seq", level_idx)
        siblings.append(received)
        if level_idx + 1 < cross_levels:
            upper_half = jnp.right_shift(where_seq, level_idx) & 1 == 1
            joined = jnp.where(
                upper_half,
                jnp.concatenate([received, current], axis=1),
                jnp.concatenate([current, received], axis=1),
            )
            current = pair_mean(joined)
    segments = [stacked.reshape(2, blocks, BLK, features)]
    for level_idx in range(local_levels):
        factor = 2**level_idx
        group_count = blocks >> level_idx
        if level_idx == 0:
            pooled = stacked
        else:
            pooled = (
                stacked.reshape(2, row_count // factor, factor, features)
                .astype(jnp.float32)
                .mean(axis=2)
                .astype(jnp.bfloat16)
            )
        paired = pooled.reshape(2, group_count // 2, 2, BLK, features)
        sibling = jnp.concatenate([paired[:, :, 1:], paired[:, :, :1]], axis=2).reshape(
            2, group_count, BLK, features
        )
        segments.append(
            jnp.broadcast_to(sibling[:, :, None], (2, group_count, factor, BLK, features)).reshape(
                2, blocks, BLK, features
            )
        )
    key_set = jnp.concatenate(segments, axis=2)
    far_set = jnp.concatenate(
        [siblings[level_idx].astype(jnp.bfloat16) for level_idx in range(cross_levels)], axis=1
    )
    near_keys = (1 + local_levels) * BLK
    far_keys = cross_levels * BLK
    key_bias = jnp.concatenate(
        [jnp.zeros((BLK,), jnp.float32)]
        + [jnp.full((BLK,), level_idx * LOG_TWO, jnp.float32) for level_idx in range(level_count)]
    )
    level_flags = pattern == 1
    kept_mask = jnp.concatenate(
        [
            jnp.ones((blocks, BLK), bool),
            jnp.broadcast_to(level_flags[:, :, None], (blocks, level_count, BLK)).reshape(
                blocks, level_count * BLK
            ),
        ],
        axis=1,
    )
    query_heads = queries.reshape(blocks, BLK, head_count, DH)
    key_heads = key_set[0].reshape(blocks, near_keys, head_count, DH)
    value_heads = key_set[1].reshape(blocks, near_keys, head_count, DH)
    far_key_heads = far_set[0].reshape(far_keys, head_count, DH)
    far_value_heads = far_set[1].reshape(far_keys, head_count, DH)
    scores = (
        jnp.concatenate(
            [
                jnp.einsum(
                    "bqhd,bkhd->bhqk", query_heads, key_heads, preferred_element_type=jnp.float32
                ),
                jnp.einsum(
                    "bqhd,khd->bhqk", query_heads, far_key_heads, preferred_element_type=jnp.float32
                ),
            ],
            axis=-1,
        )
        * score_scale
        + key_bias
    )
    scores = jnp.where(kept_mask[:, None, None, :], scores, -jnp.inf)
    row_max = jnp.max(scores, axis=-1, keepdims=True)
    weights_raw = jnp.exp(scores - row_max)
    attn_prob = weights_raw / jnp.sum(weights_raw, axis=-1, keepdims=True)
    prob_low = attn_prob.astype(jnp.bfloat16)
    near_prob, far_prob = (prob_low[..., :near_keys], prob_low[..., near_keys:])
    mixed = jnp.einsum(
        "bhqk,bkhd->bqhd", near_prob, value_heads, preferred_element_type=jnp.float32
    ) + jnp.einsum("bhqk,khd->bqhd", far_prob, far_value_heads, preferred_element_type=jnp.float32)
    attended = mixed.astype(jnp.bfloat16).reshape(row_count, features)
    attended, weight_cols = lax.optimization_barrier((attended, weight_columns(out_weight)))
    half_rows = row_count // 2
    grads_full = jnp.concatenate(
        [
            lax.all_gather(cotangent[:half_rows], "head", axis=1, tiled=True),
            head_ring_gather(cotangent[half_rows:]),
        ],
        axis=0,
    )
    grad_attn = lax.dot_general(
        grads_full, out_weight, (((1,), (1,)), ((), ())), preferred_element_type=jnp.float32
    ).astype(jnp.bfloat16)
    late_attended, grad_attn = lax.optimization_barrier((attended, grad_attn))
    attended_blocks = head_ring_gather(late_attended, relative=True)
    grad_weight = lax.psum_scatter(
        lax.dot_general(
            grads_full, attended, (((0,), (0,)), ((), ())), preferred_element_type=jnp.float32
        ),
        "seq",
        scatter_dimension=0,
        tiled=True,
    )
    grad_heads = grad_attn.reshape(blocks, BLK, head_count, DH)
    grad_prob = jnp.concatenate(
        [
            jnp.einsum(
                "bqhd,bkhd->bhqk", grad_heads, value_heads, preferred_element_type=jnp.float32
            ),
            jnp.einsum(
                "bqhd,khd->bhqk", grad_heads, far_value_heads, preferred_element_type=jnp.float32
            ),
        ],
        axis=-1,
    )
    row_delta = jnp.sum(attn_prob * grad_prob, axis=-1, keepdims=True)
    grad_score = (attn_prob * (grad_prob - row_delta)).astype(jnp.bfloat16)
    near_score, far_score = (grad_score[..., :near_keys], grad_score[..., near_keys:])
    grad_query = (
        (
            (
                jnp.einsum(
                    "bhqk,bkhd->bqhd", near_score, key_heads, preferred_element_type=jnp.float32
                )
                + jnp.einsum(
                    "bhqk,khd->bqhd", far_score, far_key_heads, preferred_element_type=jnp.float32
                )
            )
            * score_scale
        )
        .astype(jnp.bfloat16)
        .reshape(row_count, features)
    )
    grad_keyset = (
        jnp.einsum("bhqk,bqhd->bkhd", near_score, query_heads, preferred_element_type=jnp.float32)
        * score_scale
    )
    grad_valset = jnp.einsum(
        "bhqk,bqhd->bkhd", near_prob, grad_heads, preferred_element_type=jnp.float32
    )
    grad_sets = jnp.stack([grad_keyset, grad_valset]).reshape(2, blocks, near_keys, features)
    far_grad_keys = (
        jnp.einsum("bhqk,bqhd->khd", far_score, query_heads, preferred_element_type=jnp.float32)
        * score_scale
    )
    far_grad_values = jnp.einsum(
        "bhqk,bqhd->khd", far_prob, grad_heads, preferred_element_type=jnp.float32
    )
    far_grads = jnp.stack([far_grad_keys, far_grad_values]).reshape(2, far_keys, features)
    token_grad = grad_sets[:, :, :BLK].reshape(2, row_count, features)
    level_grads = []
    for level_idx in range(local_levels):
        factor = 2**level_idx
        group_count = blocks >> level_idx
        lower = (level_idx + 1) * BLK
        segment = (
            grad_sets[:, :, lower : lower + BLK]
            .reshape(2, group_count, factor, BLK, features)
            .sum(axis=2)
        )
        paired = segment.reshape(2, group_count // 2, 2, BLK, features)
        restored = jnp.concatenate([paired[:, :, 1:], paired[:, :, :1]], axis=2).reshape(
            2, group_count * BLK, features
        )
        level_grads.append(restored)
    sibling_grads = []
    for level_idx in range(cross_levels):
        sibling_grads.append(far_grads[:, level_idx * BLK : (level_idx + 1) * BLK])
    carried = jnp.zeros((2, BLK, features), jnp.float32)
    for level_idx in reversed(range(cross_levels)):
        outgoing = sibling_grads[level_idx]
        if level_idx + 1 < cross_levels:
            halves = spread_rows(carried, 2)
            lower_part = halves[:, :BLK]
            upper_part = halves[:, BLK:]
            upper_half = jnp.right_shift(where_seq, level_idx) & 1 == 1
            own_part = jnp.where(upper_half, upper_part, lower_part)
            outgoing = outgoing + jnp.where(upper_half, lower_part, upper_part)
        else:
            own_part = jnp.zeros_like(outgoing)
        carried = own_part + swapped(outgoing, "seq", level_idx)
    attended_blocks, carried = lax.optimization_barrier((attended_blocks, carried))
    output_sum = jnp.dot(attended_blocks[0], weight_cols[0], preferred_element_type=jnp.float32)
    for dist in range(1, len(attended_blocks)):
        output_sum = output_sum + jnp.dot(
            attended_blocks[dist], weight_cols[dist], preferred_element_type=jnp.float32
        )
    output = output_sum.astype(jnp.bfloat16)
    if local_levels:
        pooled_grad = level_grads[-1]
        for level_idx in reversed(range(local_levels - 1)):
            pooled_grad = level_grads[level_idx] + spread_rows(pooled_grad, 2)
        token_grad = token_grad + pooled_grad
    token_grad = token_grad + spread_rows(carried, 2**local_levels)
    grad_keys = token_grad[0].astype(jnp.bfloat16)
    grad_values = token_grad[1].astype(jnp.bfloat16)
    return (output, grad_query, grad_keys, grad_values, grad_weight)


def solution(mesh):
    placed = (
        P("seq", "head"),
        P("seq", "head"),
        P("seq", "head"),
        P("head", None),
        P("seq", "head"),
        P("seq", None),
    )
    return jax.shard_map(
        body,
        mesh=mesh,
        in_specs=placed,
        out_specs=(
            P("seq", "head"),
            P("seq", "head"),
            P("seq", "head"),
            P("seq", "head"),
            P("seq", "head"),
        ),
        check_vma=False,
    )
```

profile of v0, /device:TPU:0, one launch (start us, length us, event | category | flops | bytes accessed | tf_op | source)
XLA Modules:
  0.0 408.6 jit_solution(15762008881767522509)
XLA Ops:
  10.7 3.0 convert_reduce_fusion
  14.6 3.3 constant_dynamic-slice_fusion.4
  17.9 3.2 collective-permute-start.6
  30.9 5.8 %convert_reduce_fusion.2 = f32[2,512,512]{2,1,0:T(8,128)S(1)} fusion(bf16[1,512,2,512]{3,2,1,0:T(2,128)(2,1)S(1)} %copy-done.28, bf16[1,512,2,512]{3,2,1,0:T(2,128)(2,1)S(1)} %copy-done.27), kind=kLoop, calls=%fused_computation.42 | loop fusion | flops 2621440 | bytes 4194304 | tf_op jit(solution)/shard_map/reduce_sum | solution.py:155
  41.5 3.5 fusion.71
  45.0 6.6 %copy.194 = bf16[1,8,512,512]{2,3,1,0:T(8,128)(2,1)} copy(bf16[1,8,512,512]{3,2,1,0:T(8,128)(2,1)} %get-tuple-element.54) | data formatting | bytes 8388608 | tf_op jit(solution)/shard_map/slice | solution.py:188
  54.9 3.1 collective-permute-start.1
  58.0 4.6 %convolution_bitcast_fusion.2 = f32[8,4,128,512]{2,3,1,0:T(8,128)} fusion(bf16[8,512,4,128]{1,3,2,0:T(8,128)(2,1)S(1)} %bitcast.165, bf16[8,128,4,128]{1,3,2,0:T(8,128)(2,1)S(1)} %copy.218), kind=kOutput, calls=%fused_computation.57 | convolution fusion | flops 536870912 | bytes 13631488 | tf_op jit(solution)/shard_map/bqhd,bkhd->bhqk/dot_general | solution.py:195
  62.7 8.1 %collective-permute-done.1 = f32[2,128,512]{2,1,0:T(8,128)S(1)} collective-permute-done((f32[2,128,512]{2,1,0:T(8,128)S(1)}, f32[2,128,512]{2,1,0:T(8,128)S(1)}, u32[]{:S(2)}, u32[]{:S(2)}) %collective-permute-start.1) | collective-permute-done | bytes 524320 | tf_op jit(solution)/shard_map/ppermute | solution.py:15
  80.5 6.5 %copy.192 = bf16[1,8,512,512]{2,3,1,0:T(8,128)(2,1)} copy(bf16[1,8,512,512]{3,2,1,0:T(8,128)(2,1)} %get-tuple-element.53) | data formatting | bytes 8388608 | tf_op jit(solution)/shard_map/slice | solution.py:189
  89.6 5.5 %collective-permute-start.7 = (bf16[512,512]{1,0:T(8,128)(2,1)}, bf16[512,512]{1,0:T(8,128)(2,1)}, u32[]{:S(2)}, u32[]{:S(2)}) collective-permute-start(bf16[512,512]{1,0:T(8,128)(2,1)} %get-tuple-element.63), channel_id=1, source_target_pairs={{0,7},{1,0},{2,1},{3,2},{4,3},{5,4},{6,5},{7,6},{16,23},{17,16},{1... | collective-permute-start | bytes 1572872 | tf_op jit(solution)/shard_map/ppermute | solution.py:90
  96.4 3.7 collective-permute-start.3
  102.7 3.1 pad_maximum_fusion.10
  105.8 17.4 %collective-permute-start.8 = (bf16[4,512,512]{2,1,0:T(8,128)(2,1)}, bf16[4,512,512]{2,1,0:T(8,128)(2,1)}, u32[]{:S(2)}, u32[]{:S(2)}) collective-permute-start(bf16[4,512,512]{2,1,0:T(8,128)(2,1)} %pad_maximum_fusion.10), channel_id=1, source_target_pairs={{0,8},{8,0},{16,24},{24,16},{32,40},{40,32},{48,56},{56,48},{64,72... | collective-permute-start | bytes 6291464 | tf_op jit(solution)/shard_map/ppermute | solution.py:92
  134.2 7.9 %fusion.81 = (f32[8,4,128]{2,1,0:T(4,128)S(1)}, f32[8,4,128,1024]{2,3,1,0:T(8,128)S(1)}) fusion(f32[8,4,128,512]{2,3,1,0:T(8,128)S(1)} %convolution_bitcast_fusion.1, f32[8,4,128,512]{2,3,1,0:T(8,128)} %convolution_bitcast_fusion.2, f32[1024]{0:T(1024)S(1)} %copy-done.46, pred[8,1024]{1,0:T(8,128)(4,1)S(1)} %concatenate.89), kind=kOutput, calls=%fused_computation.168 | output fusion | flops 25166848 | bytes 33583104 | tf_op jit(solution)/shard_map/sub | solution.py:209
  142.1 4.1 %fusion.70 = bf16[8,4,128,1024]{2,3,1,0:T(8,128)(2,1)} fusion(f32[8,4,128,1024]{2,3,1,0:T(8,128)S(1)} %get-tuple-element.95, f32[8,4,128]{2,1,0:T(4,128)S(1)} %get-tuple-element.94), kind=kLoop, calls=%fused_computation.157 | loop fusion | flops 8388608 | bytes 25182208 | tf_op jit(solution)/shard_map/convert_element_type | solution.py:211
  146.2 4.2 %copy-done.12 = f32[8,4,128,1024]{2,3,1,0:T(8,128)} copy-done((f32[8,4,128,1024]{2,3,1,0:T(8,128)}, f32[8,4,128,1024]{2,3,1,0:T(8,128)S(1)}, u32[]{:S(2)}) %copy-start.12) | copy-done | bytes 16777240
  150.7 3.1 fusion.68
  154.2 3.5 fusion.40
  163.4 5.0 %gather_fusion = bf16[4,512,1024]{2,1,0:T(8,128)(2,1)} fusion(bf16[4,512,1024]{2,1,0:T(8,128)(2,1)} %pad_maximum_fusion.7, s32[1024]{0:T(1024)S(1)} %pad_clamp_fusion), kind=kCustom, calls=%fused_computation | custom fusion | bytes 8388624 | tf_op jit(solution)/shard_map/gather | solution.py:64
  168.4 6.3 %copy.211 = bf16[512,4,1024]{0,2,1:T(8,128)(2,1)} copy(bf16[512,4,1024]{2,0,1:T(8,128)(2,1)} %bitcast.179) | data formatting | bytes 8388608 | tf_op jit(solution)/shard_map/transpose | solution.py:65
  181.9 8.6 %all-gather.2.cloned.1.call-done = bf16[512,4096]{0,1:T(8,128)(2,1)} async-done(((bf16[512,512]{0,1:T(8,128)(2,1)}), bf16[512,4096]{0,1:T(8,128)(2,1)}) %all-gather.2.cloned.1.call-update) | async-done | bytes 4194320 | tf_op jit(solution)/shard_map/all_gather | solution.py:221
  190.5 9.2 %fusion.45 = bf16[1024,512]{1,0:T(8,128)(2,1)S(1)} fusion(bf16[512,4096]{1,0:T(8,128)(2,1)} %param.9, bf16[512,4096]{0,1:T(8,128)(2,1)} %bitcast.194, bf16[512,4096]{0,1:T(8,128)(2,1)} %all-gather.2.cloned.1.call-done), kind=kOutput, calls=%fused_computation.82 | convolution fusion | flops 4312268800 | bytes 13631488 | tf_op jit(solution)/shard_map/dot_general | solution.py:226
  200.7 5.1 %fusion.20 = f32[4,128,512,1]{2,1,3,0:T(8,128)} fusion(bf16[8,128,4,128]{3,2,1,0:T(4,128)(2,1)S(1)} %reshape.240, bf16[8,4,128,1024]{2,3,1,0:T(8,128)(2,1)} %fusion.70), kind=kOutput, calls=%fused_computation.37 | convolution fusion | flops 536870912 | bytes 6291456 | tf_op jit(solution)/shard_map/bhqk,bqhd->khd/dot_general | solution.py:281
  205.8 4.6 %fusion.82 = f32[8,4,128,512]{2,3,1,0:T(8,128)} fusion(bf16[8,128,4,128]{1,3,2,0:T(8,128)(2,1)S(1)} %copy.237, bf16[8,512,4,128]{1,3,2,0:T(8,128)(2,1)S(1)} %bitcast.176), kind=kOutput, calls=%fused_computation.169 | convolution fusion | flops 536870912 | bytes 13631488 | tf_op jit(solution)/shard_map/bqhd,bkhd->bhqk/dot_general | solution.py:242
  210.5 5.5 %convolution_bitcast_fusion = f32[8,4,128,512]{2,3,1,0:T(8,128)} fusion(bf16[512,4,128,1]{0,2,1,3:T(8,128)(2,1)S(1)} %bitcast.188, bf16[8,128,4,128]{1,3,2,0:T(8,128)(2,1)S(1)} %copy.237), kind=kOutput, calls=%fused_computation.55 | convolution fusion | flops 536870912 | bytes 9961472 | tf_op jit(solution)/shard_map/bqhd,khd->bhqk/dot_general | solution.py:245
  216.8 8.3 %fusion.13 = f32[4096,512]{1,0:T(8,128)} fusion(bf16[1024,512]{0,1:T(8,128)(2,1)} %bitcast.164, bf16[512,4096]{0,1:T(8,128)(2,1)S(1)} %bitcast.195, bf16[512,4096]{0,1:T(8,128)(2,1)S(1)} %copy-done.45), kind=kOutput, calls=%fused_computation.25 | convolution fusion | flops 4311744512 | bytes 17825792 | tf_op jit(solution)/shard_map/dot_general | solution.py:232
  227.0 29.6 %multiply_convert_fusion = bf16[8,4,128,1024]{2,3,1,0:T(8,128)(2,1)} fusion(f32[8,4,128,512]{2,3,1,0:T(8,128)} %convolution_bitcast_fusion, f32[8,4,128,512]{2,3,1,0:T(8,128)} %fusion.82, f32[8,4,128,1024]{2,3,1,0:T(8,128)} %copy-done.12, f32[8,4,128]{2,1,0:T(4,128)S(1)} %get-tuple-element.94), kind=kOutput, calls=%fused_computation.13 | output fusion | flops 33559552 | bytes 41959424 | tf_op jit(solution)/shard_map/sub | solution.py:252
  256.6 4.6 %fusion.49 = f32[4,512,128]{1,2,0:T(8,128)} fusion(bf16[8,128,4,128]{1,3,2,0:T(8,128)(2,1)S(1)} %copy-done.9, bf16[8,4,128,1024]{2,3,1,0:T(8,128)(2,1)} %multiply_convert_fusion), kind=kOutput, calls=%fused_computation.84 | convolution fusion | flops 537133056 | bytes 6291456 | tf_op jit(solution)/shard_map/bhqk,bqhd->khd/dot_general | solution.py:278
  263.2 3.3 collective-permute-start.19
  266.5 3.8 fusion.30
  270.2 3.5 broadcast_multiply_fusion
  273.7 7.0 %fusion.16 = (f32[2,8,128,512]{2,3,1,0:T(8,128)}, f32[2,8,128,512]{2,3,1,0:T(8,128)}, f32[2,8,128,512]{2,3,1,0:T(8,128)}, f32[2,8,128,512]{2,3,1,0:T(8,128)}) fusion(f32[1,8,512,512]{2,3,1,0:T(8,128)S(1)} %bitcast.178, f32[1,8,512,512]{2,3,1,0:T(8,128)S(1)} %bitcast.177), kind=kLoop, calls=%fused_computation.28 | loop fusion | flops 4194304 | bytes 33554432 | tf_op jit(solution)/shard_map/stack | solution.py:276
  280.8 3.6 fusion.24
  284.4 4.2 %fusion.39 = bf16[8,128,4,128]{1,3,2,0:T(8,128)(2,1)} fusion(f32[8,4,128,128]{3,2,1,0:T(8,128)S(1)} %fusion.24, bf16[512,4,128,1]{0,2,1,3:T(8,128)(2,1)S(1)} %bitcast.190, bf16[8,4,128,1024]{2,3,1,0:T(8,128)(2,1)} %multiply_convert_fusion), kind=kOutput, calls=%fused_computation.75 | convolution fusion | flops 538443776 | bytes 7864320 | tf_op jit(solution)/shard_map/bhqk,khd->bqhd/dot_general | solution.py:260
  291.0 3.6 reduce_sum.103
  305.9 4.4 %collective-permute-done.20 = f32[2,128,512]{2,1,0:T(8,128)S(1)} collective-permute-done((f32[2,128,512]{2,1,0:T(8,128)S(1)}, f32[2,128,512]{2,1,0:T(8,128)S(1)}, u32[]{:S(2)}, u32[]{:S(2)}) %collective-permute-start.20) | collective-permute-done | bytes 524320 | tf_op jit(solution)/shard_map/ppermute | solution.py:15
  312.6 3.0 collective-permute-start.21
  321.4 5.4 %copy.239 = f32[2,8,128,512]{3,2,1,0:T(8,128)} copy(f32[2,8,128,512]{2,3,1,0:T(8,128)} %get-tuple-element.49) | data formatting | bytes 8388608 | tf_op jit(solution)/shard_map/slice | solution.py:285
  329.7 4.1 reduce_sum.102
  336.3 3.1 fusion.73
  344.5 3.3 broadcast_in_dim.44
  347.7 3.6 reshape.253
  365.3 3.5 broadcast_in_dim.45
  368.8 6.3 %reshape.254 = f32[2,1024,512]{2,1,0:T(8,128)} reshape(f32[2,512,2,512]{3,2,1,0:T(2,128)} %broadcast_in_dim.45) | data formatting | bytes 8388608 | tf_op jit(solution)/shard_map/reshape | solution.py:29
  390.3 3.0 fusion.83
  393.3 3.0 fusion.84
  397.6 3.9 add_convert_fusion
  (236 shorter events, 130.7 us)
Async XLA Ops:
  7.2 183.4 %all-gather.2.cloned.1.call-start = ((), (), s32[]{:S(2)}) async-start(), calls=%async_computation.1 | async-start | bytes 4718592 | tf_op jit(solution)/shard_map/all_gather | solution.py:221
  9.1 65.8 %collective-permute-start.9 = (bf16[512,512]{1,0:T(8,128)(2,1)}, bf16[512,512]{1,0:T(8,128)(2,1)}, u32[]{:S(2)}, u32[]{:S(2)}) collective-permute-start(bf16[512,512]{1,0:T(8,128)(2,1)} %slice.169), channel_id=1, source_target_pairs={{0,1},{1,0},{2,3},{3,2},{4,5},{5,4},{6,7},{7,6},{8,9},{9,8},{10,11... | collective-permute-start | bytes 1572872 | tf_op jit(solution)/shard_map/ppermute | solution.py:38
  10.7 10.4 %copy-start.3 = (bf16[1024,512]{1,0:T(8,128)(2,1)S(1)}, bf16[1024,512]{1,0:T(8,128)(2,1)}, u32[]{:S(2)}) copy-start(bf16[1024,512]{1,0:T(8,128)(2,1)} %param.7) | copy-start | bytes 3145732
  14.6 37.1 %collective-permute-start = (f32[2,128,512]{2,1,0:T(8,128)}, f32[2,128,512]{2,1,0:T(8,128)}, u32[]{:S(2)}, u32[]{:S(2)}) collective-permute-start(f32[2,128,512]{2,1,0:T(8,128)} %broadcast_multiply_fusion.3), channel_id=1, source_target_pairs={{0,8},{8,0},{16,24},{24,16},{32,40},{40,32},{48,56},{56,48},{64,72... | collective-permute-start | bytes 1572872 | tf_op jit(solution)/shard_map/ppermute | solution.py:15
  14.6 9.3 %copy-start.2 = (bf16[1024,512]{1,0:T(8,128)(2,1)S(1)}, bf16[1024,512]{1,0:T(8,128)(2,1)}, u32[]{:S(2)}) copy-start(bf16[1024,512]{1,0:T(8,128)(2,1)} %param.8) | copy-start | bytes 3145732
  17.9 71.7 %collective-permute-start.6 = (bf16[512,512]{1,0:T(8,128)(2,1)}, bf16[512,512]{1,0:T(8,128)(2,1)}, u32[]{:S(2)}, u32[]{:S(2)}) collective-permute-start(bf16[512,512]{1,0:T(8,128)(2,1)} %get-tuple-element.60), channel_id=1, source_target_pairs={{0,5},{1,6},{2,7},{3,0},{4,1},{5,2},{6,3},{7,4},{8,14},{9,15},{10,... | collective-permute-start | bytes 1572872 | tf_op jit(solution)/shard_map/ppermute | solution.py:90
  21.1 75.3 %collective-permute-start.5 = (bf16[512,512]{1,0:T(8,128)(2,1)}, bf16[512,512]{1,0:T(8,128)(2,1)}, u32[]{:S(2)}, u32[]{:S(2)}) collective-permute-start(bf16[512,512]{1,0:T(8,128)(2,1)} %get-tuple-element.61), channel_id=1, source_target_pairs={{0,3},{1,4},{2,5},{3,6},{4,7},{5,0},{6,1},{7,2},{8,12},{9,13},{10,... | collective-permute-start | bytes 1572872 | tf_op jit(solution)/shard_map/ppermute | solution.py:90
  29.0 103.9 %copy-start.8 = (bf16[8,128,4,128]{1,3,2,0:T(8,128)(2,1)}, bf16[8,128,4,128]{1,3,2,0:T(8,128)(2,1)S(1)}, u32[]{:S(2)}) copy-start(bf16[8,128,4,128]{1,3,2,0:T(8,128)(2,1)S(1)} %copy.218) | copy-start | bytes 3145732
  51.7 6.3 %copy-start = (bf16[1,8,512,512]{2,3,1,0:T(8,128)(2,1)S(1)}, bf16[1,8,512,512]{2,3,1,0:T(8,128)(2,1)}, u32[]{:S(2)}) copy-start(bf16[1,8,512,512]{2,3,1,0:T(8,128)(2,1)} %copy.194) | copy-start | bytes 12582916
  54.9 15.8 %collective-permute-start.1 = (f32[2,128,512]{2,1,0:T(8,128)S(1)}, f32[2,128,512]{2,1,0:T(8,128)S(1)}, u32[]{:S(2)}, u32[]{:S(2)}) collective-permute-start(f32[2,128,512]{2,1,0:T(8,128)S(1)} %copy_multiply_fusion.2), channel_id=1, source_target_pairs={{0,16},{8,24},{16,0},{24,8},{32,48},{40,56},{48,32},{56,40},{64,80... | collective-permute-start | bytes 1572872 | tf_op jit(solution)/shard_map/ppermute | solution.py:15
  62.7 12.2 %copy-start.30 = (bf16[1024,512]{1,0:T(8,128)(2,1)S(1)}, bf16[1024,512]{1,0:T(8,128)(2,1)}, u32[]{:S(2)}) copy-start(bf16[1024,512]{1,0:T(8,128)(2,1)} %param.10) | copy-start | bytes 3145732
  70.7 7.7 %copy-start.35 = (f32[2,128,512]{2,1,0:T(8,128)}, f32[2,128,512]{2,1,0:T(8,128)S(1)}, u32[]{:S(2)}) copy-start(f32[2,128,512]{2,1,0:T(8,128)S(1)} %collective-permute-done.1) | copy-start | bytes 1572868
  73.0 14.0 %collective-permute-start.2 = (f32[2,128,512]{2,1,0:T(8,128)}, f32[2,128,512]{2,1,0:T(8,128)}, u32[]{:S(2)}, u32[]{:S(2)}) collective-permute-start(f32[2,128,512]{2,1,0:T(8,128)} %copy_multiply_fusion.1), channel_id=1, source_target_pairs={{0,32},{8,40},{16,48},{24,56},{32,0},{40,8},{48,16},{56,24},{64,96... | collective-permute-start | bytes 1572872 | tf_op jit(solution)/shard_map/ppermute | solution.py:15
  78.4 45.9 %collective-permute-start.10 = (bf16[512,1024]{1,0:T(8,128)(2,1)}, bf16[512,1024]{1,0:T(8,128)(2,1)S(1)}, u32[]{:S(2)}, u32[]{:S(2)}) collective-permute-start(bf16[512,1024]{1,0:T(8,128)(2,1)} %get-tuple-element.87), channel_id=1, source_target_pairs={{0,6},{1,7},{2,0},{3,1},{4,2},{5,3},{6,4},{7,5},{8,14},{9,15},{10,... | collective-permute-start | bytes 3145736 | tf_op jit(solution)/shard_map/ppermute | solution.py:49
  79.5 47.8 %collective-permute-start.11 = (bf16[512,1024]{1,0:T(8,128)(2,1)}, bf16[512,1024]{1,0:T(8,128)(2,1)S(1)}, u32[]{:S(2)}, u32[]{:S(2)}) collective-permute-start(bf16[512,1024]{1,0:T(8,128)(2,1)} %get-tuple-element.87), channel_id=1, source_target_pairs={{0,2},{1,3},{2,4},{3,5},{4,6},{5,7},{6,0},{7,1},{8,10},{9,11},{10,... | collective-permute-start | bytes 3145736 | tf_op jit(solution)/shard_map/ppermute | solution.py:48
  87.0 15.2 %collective-permute-start.4 = (bf16[512,512]{1,0:T(8,128)(2,1)}, bf16[512,512]{1,0:T(8,128)(2,1)}, u32[]{:S(2)}, u32[]{:S(2)}) collective-permute-start(bf16[512,512]{1,0:T(8,128)(2,1)} %get-tuple-element.62), channel_id=1, source_target_pairs={{0,1},{1,2},{2,3},{3,4},{4,5},{5,6},{6,7},{7,0},{8,10},{9,11},{10,... | collective-permute-start | bytes 1572872 | tf_op jit(solution)/shard_map/ppermute | solution.py:90
  89.6 13.1 %collective-permute-start.7 = (bf16[512,512]{1,0:T(8,128)(2,1)}, bf16[512,512]{1,0:T(8,128)(2,1)}, u32[]{:S(2)}, u32[]{:S(2)}) collective-permute-start(bf16[512,512]{1,0:T(8,128)(2,1)} %get-tuple-element.63), channel_id=1, source_target_pairs={{0,7},{1,0},{2,1},{3,2},{4,3},{5,4},{6,5},{7,6},{16,23},{17,16},{1... | collective-permute-start | bytes 1572872 | tf_op jit(solution)/shard_map/ppermute | solution.py:90
  96.4 33.1 %collective-permute-start.3 = (bf16[2,128,512]{2,1,0:T(8,128)(2,1)S(1)}, bf16[2,128,512]{2,1,0:T(8,128)(2,1)}, u32[]{:S(2)}, u32[]{:S(2)}) collective-permute-start(bf16[2,128,512]{2,1,0:T(8,128)(2,1)S(1)} %copy_multiply_fusion), channel_id=1, source_target_pairs={{0,64},{8,72},{16,80},{24,88},{32,96},{40,104},{48,112},{56,120},{... | collective-permute-start | bytes 786440 | tf_op jit(solution)/shard_map/ppermute | solution.py:15
  102.2 299.3 %reduce-scatter.2.cloned.1.call-start = ((), (), s32[]{:S(2)}) async-start(), calls=%async_computation.2 | async-start | bytes 8912896 | tf_op jit(solution)/shard_map/reduce_scatter | solution.py:231
  102.2 22.1 %copy-start.36 = (f32[2,128,512]{2,1,0:T(8,128)S(1)}, f32[2,128,512]{2,1,0:T(8,128)}, u32[]{:S(2)}) copy-start(f32[2,128,512]{2,1,0:T(8,128)} %copy-done.35) | copy-start | bytes 1572868
  105.8 68.8 %collective-permute-start.8 = (bf16[4,512,512]{2,1,0:T(8,128)(2,1)}, bf16[4,512,512]{2,1,0:T(8,128)(2,1)}, u32[]{:S(2)}, u32[]{:S(2)}) collective-permute-start(bf16[4,512,512]{2,1,0:T(8,128)(2,1)} %pad_maximum_fusion.10), channel_id=1, source_target_pairs={{0,8},{8,0},{16,24},{24,16},{32,40},{40,32},{48,56},{56,48},{64,72... | collective-permute-start | bytes 6291464 | tf_op jit(solution)/shard_map/ppermute | solution.py:92
  124.3 7.2 %copy-start.31 = (bf16[512,1024]{1,0:T(8,128)(2,1)}, bf16[512,1024]{1,0:T(8,128)(2,1)S(1)}, u32[]{:S(2)}) copy-start(bf16[512,1024]{1,0:T(8,128)(2,1)S(1)} %collective-permute-done.10) | copy-start | bytes 3145732
  125.3 34.3 %collective-permute-start.13 = (bf16[512,512]{1,0:T(8,128)(2,1)}, bf16[512,512]{1,0:T(8,128)(2,1)}, u32[]{:S(2)}, u32[]{:S(2)}) collective-permute-start(bf16[512,512]{1,0:T(8,128)(2,1)} %slice.220), channel_id=1, source_target_pairs={{0,6},{1,7},{2,0},{3,1},{4,2},{5,3},{6,4},{7,5},{8,14},{9,15},{10,... | collective-permute-start | bytes 1572872 | tf_op jit(solution)/shard_map/ppermute | solution.py:55
  127.3 6.9 %copy-start.33 = (bf16[512,1024]{1,0:T(8,128)(2,1)}, bf16[512,1024]{1,0:T(8,128)(2,1)S(1)}, u32[]{:S(2)}) copy-start(bf16[512,1024]{1,0:T(8,128)(2,1)S(1)} %collective-permute-done.11) | copy-start | bytes 3145732
  128.2 31.5 %collective-permute-start.12 = (bf16[512,512]{1,0:T(8,128)(2,1)}, bf16[512,512]{1,0:T(8,128)(2,1)}, u32[]{:S(2)}, u32[]{:S(2)}) collective-permute-start(bf16[512,512]{1,0:T(8,128)(2,1)} %slice.219), channel_id=1, source_target_pairs={{0,2},{1,3},{2,4},{3,5},{4,6},{5,7},{6,0},{7,1},{8,10},{9,11},{10,... | collective-permute-start | bytes 1572872 | tf_op jit(solution)/shard_map/ppermute | solution.py:54
  142.1 8.4 %copy-start.12 = (f32[8,4,128,1024]{2,3,1,0:T(8,128)}, f32[8,4,128,1024]{2,3,1,0:T(8,128)S(1)}, u32[]{:S(2)}) copy-start(f32[8,4,128,1024]{2,3,1,0:T(8,128)S(1)} %get-tuple-element.95) | copy-start | bytes 50331652
  142.1 8.4 %copy-start.38 = (bf16[1,512,512]{2,1,0:T(8,128)(2,1)S(1)}, bf16[1,512,512]{2,1,0:T(8,128)(2,1)}, u32[]{:S(2)}) copy-start(bf16[1,512,512]{2,1,0:T(8,128)(2,1)} %get-tuple-element.91) | copy-start | bytes 1572868
  200.7 15.2 %copy-start.11 = (bf16[8,128,4,128]{1,3,2,0:T(8,128)(2,1)}, bf16[8,128,4,128]{1,3,2,0:T(8,128)(2,1)S(1)}, u32[]{:S(2)}) copy-start(bf16[8,128,4,128]{1,3,2,0:T(8,128)(2,1)S(1)} %copy.237) | copy-start | bytes 3145732
  210.4 6.3 %copy-start.45 = (bf16[512,4096]{0,1:T(8,128)(2,1)S(1)}, bf16[512,4096]{0,1:T(8,128)(2,1)}, u32[]{:S(2)}) copy-start(bf16[512,4096]{0,1:T(8,128)(2,1)} %all-gather.2.cloned.1.call-done) | copy-start | bytes 12582916
  226.6 30.0 %copy-start.9 = (bf16[8,128,4,128]{1,3,2,0:T(8,128)(2,1)S(1)}, bf16[8,128,4,128]{1,3,2,0:T(8,128)(2,1)}, u32[]{:S(2)}) copy-start(bf16[8,128,4,128]{1,3,2,0:T(8,128)(2,1)} %copy-done.8) | copy-start | bytes 3145732
  226.6 73.5 %collective-permute-start.14 = (bf16[1024,512]{0,1:T(8,128)(2,1)}, bf16[1024,512]{0,1:T(8,128)(2,1)}, u32[]{:S(2)}, u32[]{:S(2)}) collective-permute-start(bf16[1024,512]{0,1:T(8,128)(2,1)} %bitcast.164), channel_id=1, source_target_pairs={{0,1},{1,0},{2,3},{3,2},{4,5},{5,4},{6,7},{7,6},{8,9},{9,8},{10,11... | collective-permute-start | bytes 3145736 | tf_op jit(solution)/shard_map/ppermute | solution.py:38
  263.1 7.1 %copy-start.6 = (f32[1,512,512]{2,1,0:T(8,128)}, f32[1,512,512]{2,1,0:T(8,128)S(1)}, u32[]{:S(2)}) copy-start(f32[1,512,512]{2,1,0:T(8,128)S(1)} %copy.221) | copy-start | bytes 3145732
  263.1 7.1 %copy-start.10 = (bf16[8,128,4,128]{1,3,2,0:T(8,128)(2,1)S(1)}, bf16[8,128,4,128]{1,3,2,0:T(8,128)(2,1)}, u32[]{:S(2)}) copy-start(bf16[8,128,4,128]{1,3,2,0:T(8,128)(2,1)} %copy-done.8) | copy-start | bytes 3145732
  263.2 31.5 %collective-permute-start.19 = (f32[2,128,512]{2,1,0:T(8,128)S(1)}, f32[2,128,512]{2,1,0:T(8,128)}, u32[]{:S(2)}, u32[]{:S(2)}) collective-permute-start(f32[2,128,512]{2,1,0:T(8,128)S(1)} %fusion.56), channel_id=1, source_target_pairs={{0,64},{8,72},{16,80},{24,88},{32,96},{40,104},{48,112},{56,120},{... | collective-permute-start | bytes 1572872 | tf_op jit(solution)/shard_map/ppermute | solution.py:15
  273.7 7.1 %copy-start.1 = (bf16[1,8,512,512]{2,3,1,0:T(8,128)(2,1)S(1)}, bf16[1,8,512,512]{2,3,1,0:T(8,128)(2,1)}, u32[]{:S(2)}) copy-start(bf16[1,8,512,512]{2,3,1,0:T(8,128)(2,1)} %copy.194) | copy-start | bytes 12582916
  296.9 8.9 %copy-start.26 = (f32[2,2,128,512]{2,3,1,0:T(8,128)S(1)}, f32[2,2,128,512]{2,3,1,0:T(8,128)}, u32[]{:S(2)}) copy-start(f32[2,2,128,512]{2,3,1,0:T(8,128)} %reduce_sum.103) | copy-start | bytes 3145732
  297.1 13.1 %collective-permute-start.20 = (f32[2,128,512]{2,1,0:T(8,128)S(1)}, f32[2,128,512]{2,1,0:T(8,128)S(1)}, u32[]{:S(2)}, u32[]{:S(2)}) collective-permute-start(f32[2,128,512]{2,1,0:T(8,128)S(1)} %fusion.58), channel_id=1, source_target_pairs={{0,32},{8,40},{16,48},{24,56},{32,0},{40,8},{48,16},{56,24},{64,96... | collective-permute-start | bytes 1572872 | tf_op jit(solution)/shard_map/ppermute | solution.py:15
  302.4 53.1 %collective-permute-start.16 = (bf16[1024,1024]{0,1:T(8,128)(2,1)}, bf16[1024,1024]{0,1:T(8,128)(2,1)}, u32[]{:S(2)}, u32[]{:S(2)}) collective-permute-start(bf16[1024,1024]{0,1:T(8,128)(2,1)} %constant_dynamic-update-slice_fusion), channel_id=1, source_target_pairs={{0,2},{1,3},{2,4},{3,5},{4,6},{5,7},{6,0},{7,1},{8,10},{9,11},{10,... | collective-permute-start | bytes 6291464 | tf_op jit(solution)/shard_map/ppermute | solution.py:48
  303.9 55.6 %collective-permute-start.15 = (bf16[1024,1024]{0,1:T(8,128)(2,1)}, bf16[1024,1024]{0,1:T(8,128)(2,1)}, u32[]{:S(2)}, u32[]{:S(2)}) collective-permute-start(bf16[1024,1024]{0,1:T(8,128)(2,1)} %constant_dynamic-update-slice_fusion), channel_id=1, source_target_pairs={{0,6},{1,7},{2,0},{3,1},{4,2},{5,3},{6,4},{7,5},{8,14},{9,15},{10,... | collective-permute-start | bytes 6291464 | tf_op jit(solution)/shard_map/ppermute | solution.py:49
  312.6 40.5 %collective-permute-start.21 = (f32[2,128,512]{2,1,0:T(8,128)}, f32[2,128,512]{2,1,0:T(8,128)}, u32[]{:S(2)}, u32[]{:S(2)}) collective-permute-start(f32[2,128,512]{2,1,0:T(8,128)} %fusion.55), channel_id=1, source_target_pairs={{0,16},{8,24},{16,0},{24,8},{32,48},{40,56},{48,32},{56,40},{64,80... | collective-permute-start | bytes 1572872 | tf_op jit(solution)/shard_map/ppermute | solution.py:15
  355.5 9.8 %copy-start.18 = (f32[2,128,512]{2,0,1:T(2,128)}, f32[2,128,512]{2,0,1:T(2,128)S(1)}, u32[]{:S(2)}) copy-start(f32[2,128,512]{2,0,1:T(2,128)S(1)} %get-tuple-element.80) | copy-start | bytes 1572868
  355.5 9.3 %copy-start.16 = (f32[2,512,512]{2,1,0:T(8,128)S(1)}, f32[2,512,512]{2,1,0:T(8,128)}, u32[]{:S(2)}) copy-start(f32[2,512,512]{2,1,0:T(8,128)} %reshape.253) | copy-start | bytes 6291460
  358.0 24.7 %collective-permute-start.17 = (bf16[1024,512]{0,1:T(8,128)(2,1)}, bf16[1024,512]{0,1:T(8,128)(2,1)}, u32[]{:S(2)}, u32[]{:S(2)}) collective-permute-start(bf16[1024,512]{0,1:T(8,128)(2,1)} %slice.221), channel_id=1, source_target_pairs={{0,2},{1,3},{2,4},{3,5},{4,6},{5,7},{6,0},{7,1},{8,10},{9,11},{10,... | collective-permute-start | bytes 3145736 | tf_op jit(solution)/shard_map/ppermute | solution.py:54
  361.7 23.3 %collective-permute-start.18 = (bf16[1024,512]{0,1:T(8,128)(2,1)}, bf16[1024,512]{0,1:T(8,128)(2,1)}, u32[]{:S(2)}, u32[]{:S(2)}) collective-permute-start(bf16[1024,512]{0,1:T(8,128)(2,1)} %slice.222), channel_id=1, source_target_pairs={{0,6},{1,7},{2,0},{3,1},{4,2},{5,3},{6,4},{7,5},{8,14},{9,15},{10,... | collective-permute-start | bytes 3145736 | tf_op jit(solution)/shard_map/ppermute | solution.py:55
  364.5 15.3 %collective-permute-start.22 = (f32[2,128,512]{2,1,0:T(8,128)}, f32[2,128,512]{2,1,0:T(8,128)S(1)}, u32[]{:S(2)}, u32[]{:S(2)}) collective-permute-start(f32[2,128,512]{2,1,0:T(8,128)} %fusion.59), channel_id=1, source_target_pairs={{0,8},{8,0},{16,24},{24,16},{32,40},{40,32},{48,56},{56,48},{64,72... | collective-permute-start | bytes 1572872 | tf_op jit(solution)/shard_map/ppermute | solution.py:15
  368.8 6.3 %copy-start.17 = (f32[2,4,1,128,512]{3,4,2,1,0:T(8,128)S(1)}, f32[2,4,1,128,512]{3,4,2,1,0:T(8,128)}, u32[]{:S(2)}) copy-start(f32[2,4,1,128,512]{3,4,2,1,0:T(8,128)} %get-tuple-element.56) | copy-start | bytes 6291460
  376.9 9.9 %copy-start.14 = (f32[2,1024,512]{2,1,0:T(8,128)S(1)}, f32[2,1024,512]{2,1,0:T(8,128)}, u32[]{:S(2)}) copy-start(f32[2,1024,512]{2,1,0:T(8,128)} %reshape.254) | copy-start | bytes 12582916
  379.8 7.0 %copy-start.13 = (f32[2,8,128,512]{3,2,1,0:T(8,128)S(1)}, f32[2,8,128,512]{3,2,1,0:T(8,128)}, u32[]{:S(2)}) copy-start(f32[2,8,128,512]{3,2,1,0:T(8,128)} %copy.239) | copy-start | bytes 12582916
  (24 other events, 77.4 us)
Sparse Core Ops, SparseCore 0:
  102.3 88.2 all-gather.1
  225.2 113.2 reduce-scatter.1
where the time goes:
time: 414 us; the launch traced here: 409 us
  local copies, waits for them, and re-layouts  120 us (29%)
  other arithmetic  115 us (28%)
  matrix products  76 us (18%)
  starting transfers between devices  55.5 us (13%)
  waiting for transfers between devices  26.6 us (6%)
  between operations  15.3 us (4%)
    sub x1, other arithmetic, body(): grad_score = (attn_prob * (grad_prob - row_delta)).astype(jnp.bfloat16)  29.6 us
    unnamed x103, local copies, waits for them, and re-layouts  28.6 us
    ppermute x1, starting transfers between devices, weight_columns(): lax.ppermute(mine, 'seq', [(src, src ^ 1) for src in range(seq_count)])  17.4 us
    ppermute x8, starting transfers between devices, swapped(): return lax.ppermute(value, axis, pairs)  15.9 us
    ppermute x8, waiting for transfers between devices, swapped(): return lax.ppermute(value, axis, pairs)  12.5 us
    slice x2, local copies, waits for them, and re-layouts, body(): value_heads = key_set[1].reshape(blocks, near_keys, head_count, DH)  10 us
    reshape x2, local copies, waits for them, and re-layouts, spread_rows(): return wide.reshape(shape_in[:-2] + (shape_in[-2] * factor, shape_in[-1]))  9.9 us
    ppermute x4, starting transfers between devices, weight_columns(): fetched.append(lax.ppermute(outgoing, ('seq', 'head'), pairs))  9.28 us
  transfers between devices with their start and end apart: 25, of which 6 were waited for; matrix products, arithmetic and copies ran while one was open for 65% of the time, Pallas kernels for 0%

commit v1 on v0

--- a/solution.py
+++ b/solution.py
@@ -7,6 +7,14 @@
 DH = 128
 BLK = 128
 LOG_TWO = math.log(2.0)
+
+
+def do_tiles(x_part):
+    m_next = jnp.stack([x_part for _ in range(lax.axis_size("head"))], axis=0)
+    kept_arr = jnp.concatenate(
+        lax.all_to_all(m_next, axis_name="head", split_axis=0, concat_axis=0), axis=1
+    )
+    return kept_arr
 
 
 def swapped(value, axis, bit):
@@ -217,11 +225,7 @@
     attended, weight_cols = lax.optimization_barrier((attended, weight_columns(out_weight)))
     half_rows = row_count // 2
     grads_full = jnp.concatenate(
-        [
-            lax.all_gather(cotangent[:half_rows], "head", axis=1, tiled=True),
-            head_ring_gather(cotangent[half_rows:]),
-        ],
-        axis=0,
+        [do_tiles(cotangent[:half_rows]), head_ring_gather(cotangent[half_rows:])], axis=0
     )
     grad_attn = lax.dot_general(
         grads_full, out_weight, (((1,), (1,)), ((), ())), preferred_element_type=jnp.float32

time: 414 us -> 435 us (1.051)
  waiting for transfers between devices: 26.6 us -> 42.5 us
    ppermute x2, waiting for transfers between devices: 2.3 us -> 23.9 us  [head_ring_gather(): lax.ppermute(from_above[..., width:], 'head', downward)]
    all_gather x1 -> x0, waiting for transfers between devices: 8.63 us -> none  [body(): lax.all_gather(cotangent[:half_rows], 'head', axis=1, tiled=True)]
    unnamed x103 -> x102, local copies, waits for them, and re-layouts: 28.6 us -> 22.5 us
    all_to_all x0 -> x1, starting transfers between devices: none -> 4.55 us  [do_tiles(): lax.all_to_all(m_next, axis_name='head', split_axis=0, concat_axis=0)]
    ppermute x1, starting transfers between devices: 17.4 us -> 12.9 us  [weight_columns(): lax.ppermute(mine, 'seq', [(src, src ^ 1) for src in range(seq_count)])]
  transfers between devices with their start and end apart: 25 -> 25, of which waited for: 6 -> 7; matrix products, arithmetic and copies ran while one was open for 65% -> 63% of each run, Pallas kernels for 0% -> 0%
where the time goes in v1:
time: 435 us; the launch traced here: 429 us
  local copies, waits for them, and re-layouts  121 us (28%)
  other arithmetic  116 us (27%)
  matrix products  78 us (18%)
  starting transfers between devices  56.9 us (13%)
  waiting for transfers between devices  42.5 us (10%)
  between operations  15.5 us (4%)
    sub x1, other arithmetic, body(): grad_score = (attn_prob * (grad_prob - row_delta)).astype(jnp.bfloat16)  29.3 us
    ppermute x2, waiting for transfers between devices, head_ring_gather(): lax.ppermute(from_above[..., width:], 'head', downward)  23.9 us
    unnamed x102, local copies, waits for them, and re-layouts  22.5 us
    ppermute x8, starting transfers between devices, swapped(): return lax.ppermute(value, axis, pairs)  15.2 us
    ppermute x8, waiting for transfers between devices, swapped(): return lax.ppermute(value, axis, pairs)  14.2 us
    ppermute x1, starting transfers between devices, weight_columns(): lax.ppermute(mine, 'seq', [(src, src ^ 1) for src in range(seq_count)])  12.9 us
    dot_general x1, matrix products, body(): lax.dot_general(grads_full, out_weight, (((1,), (1,)), ((), ())), preferr...  10.3 us
    reshape x2, local copies, waits for them, and re-layouts, spread_rows(): return wide.reshape(shape_in[:-2] + (shape_in[-2] * factor, shape_in[-1]))  10.2 us
  transfers between devices with their start and end apart: 25, of which 7 were waited for; matrix products, arithmetic and copies ran while one was open for 63% of the time, Pallas kernels for 0%

profile of v1, /device:TPU:0, one launch (start us, length us, event | category | flops | bytes accessed | tf_op | source)
XLA Modules:
  0.0 429.3 jit_solution(14866917458677267746)
XLA Ops:
  10.7 3.0 convert_reduce_fusion
  14.5 3.3 constant_dynamic-slice_fusion.4
  17.8 3.2 collective-permute-start.6
  30.9 5.8 %convert_reduce_fusion.2 = f32[2,512,512]{2,1,0:T(8,128)S(1)} fusion(bf16[1,512,2,512]{3,2,1,0:T(2,128)(2,1)S(1)} %copy-done.30, bf16[1,512,2,512]{3,2,1,0:T(2,128)(2,1)S(1)} %copy-done.29), kind=kLoop, calls=%fused_computation.42 | loop fusion | flops 2621440 | bytes 4194304 | tf_op jit(solution)/shard_map/reduce_sum | solution.py:163
  41.5 3.6 fusion.71
  45.0 6.6 %copy.194 = bf16[1,8,512,512]{2,3,1,0:T(8,128)(2,1)} copy(bf16[1,8,512,512]{3,2,1,0:T(8,128)(2,1)} %get-tuple-element.54) | data formatting | bytes 8388608 | tf_op jit(solution)/shard_map/slice | solution.py:196
  54.9 3.1 collective-permute-start.1
  58.0 4.6 %convolution_bitcast_fusion.2 = f32[8,4,128,512]{2,3,1,0:T(8,128)} fusion(bf16[8,512,4,128]{1,3,2,0:T(8,128)(2,1)S(1)} %bitcast.168, bf16[8,128,4,128]{1,3,2,0:T(8,128)(2,1)S(1)} %copy.218), kind=kOutput, calls=%fused_computation.57 | convolution fusion | flops 536870912 | bytes 13631488 | tf_op jit(solution)/shard_map/bqhd,bkhd->bhqk/dot_general | solution.py:203
  62.6 8.1 %collective-permute-done.1 = f32[2,128,512]{2,1,0:T(8,128)S(1)} collective-permute-done((f32[2,128,512]{2,1,0:T(8,128)S(1)}, f32[2,128,512]{2,1,0:T(8,128)S(1)}, u32[]{:S(2)}, u32[]{:S(2)}) %collective-permute-start.1) | collective-permute-done | bytes 524320 | tf_op jit(solution)/shard_map/ppermute | solution.py:23
  80.5 6.5 %copy.192 = bf16[1,8,512,512]{2,3,1,0:T(8,128)(2,1)} copy(bf16[1,8,512,512]{3,2,1,0:T(8,128)(2,1)} %get-tuple-element.53) | data formatting | bytes 8388608 | tf_op jit(solution)/shard_map/slice | solution.py:197
  89.4 5.5 %collective-permute-start.7 = (bf16[512,512]{1,0:T(8,128)(2,1)}, bf16[512,512]{1,0:T(8,128)(2,1)}, u32[]{:S(2)}, u32[]{:S(2)}) collective-permute-start(bf16[512,512]{1,0:T(8,128)(2,1)} %get-tuple-element.63), channel_id=1, source_target_pairs={{0,7},{1,0},{2,1},{3,2},{4,3},{5,4},{6,5},{7,6},{16,23},{17,16},{1... | collective-permute-start | bytes 1572872 | tf_op jit(solution)/shard_map/ppermute | solution.py:98
  96.2 3.7 collective-permute-start.3
  102.6 3.1 pad_maximum_fusion.10
  105.7 12.9 %collective-permute-start.8 = (bf16[4,512,512]{2,1,0:T(8,128)(2,1)}, bf16[4,512,512]{2,1,0:T(8,128)(2,1)}, u32[]{:S(2)}, u32[]{:S(2)}) collective-permute-start(bf16[4,512,512]{2,1,0:T(8,128)(2,1)} %pad_maximum_fusion.10), channel_id=1, source_target_pairs={{0,8},{8,0},{16,24},{24,16},{32,40},{40,32},{48,56},{56,48},{64,72... | collective-permute-start | bytes 6291464 | tf_op jit(solution)/shard_map/ppermute | solution.py:100
  121.0 4.6 %all-to-all-start = ((bf16[8,512,512]{1,2,0:T(8,128)(2,1)}), bf16[8,512,512]{1,2,0:T(8,128)(2,1)}, u32[]{:S(2)}, u32[]{:S(2)}) async-start(bf16[8,512,512]{1,2,0:T(8,128)(2,1)} %stack.112), calls=%async_computation | async-start | bytes 8388608 | tf_op jit(solution)/shard_map/all_to_all | solution.py:15
  128.7 3.1 collective-permute-start.13
  138.7 7.8 %fusion.81 = (f32[8,4,128]{2,1,0:T(4,128)S(1)}, f32[8,4,128,1024]{2,3,1,0:T(8,128)S(1)}) fusion(f32[8,4,128,512]{2,3,1,0:T(8,128)S(1)} %convolution_bitcast_fusion.1, f32[8,4,128,512]{2,3,1,0:T(8,128)} %convolution_bitcast_fusion.2, f32[1024]{0:T(1024)S(1)} %copy-done.46, pred[8,1024]{1,0:T(8,128)(4,1)S(1)} %concatenate.89), kind=kOutput, calls=%fused_computation.168 | output fusion | flops 25166848 | bytes 33583104 | tf_op jit(solution)/shard_map/sub | solution.py:217
  146.5 4.1 fusion.70
  150.6 4.2 copy-done.12
  155.0 3.1 fusion.68
  158.5 3.5 fusion.40
  162.9 21.6 %collective-permute-done.13 = bf16[512,512]{1,0:T(8,128)(2,1)} collective-permute-done((bf16[512,512]{1,0:T(8,128)(2,1)}, bf16[512,512]{1,0:T(8,128)(2,1)}, u32[]{:S(2)}, u32[]{:S(2)}) %collective-permute-start.13) | collective-permute-done | bytes 524320 | tf_op jit(solution)/shard_map/ppermute | solution.py:63
  189.4 5.0 %gather_fusion = bf16[4,512,1024]{2,1,0:T(8,128)(2,1)} fusion(bf16[4,512,1024]{2,1,0:T(8,128)(2,1)} %pad_maximum_fusion.7, s32[1024]{0:T(1024)S(1)} %pad_clamp_fusion), kind=kCustom, calls=%fused_computation | custom fusion | bytes 8388624 | tf_op jit(solution)/shard_map/gather | solution.py:72
  194.4 6.2 %copy.211 = bf16[512,4,1024]{0,2,1:T(8,128)(2,1)} copy(bf16[512,4,1024]{2,0,1:T(8,128)(2,1)} %bitcast.182) | data formatting | bytes 8388608 | tf_op jit(solution)/shard_map/transpose | solution.py:73
  207.8 10.3 %fusion.45 = bf16[1024,512]{1,0:T(8,128)(2,1)} fusion(bf16[512,4096]{1,0:T(8,128)(2,1)} %param.9, bf16[512,4096]{0,1:T(8,128)(2,1)} %bitcast.197, bf16[512,4096]{0,1:T(8,128)(2,1)} %bitcast.39), kind=kOutput, calls=%fused_computation.82 | convolution fusion | flops 4312268800 | bytes 13631488 | tf_op jit(solution)/shard_map/dot_general | solution.py:230
  218.1 10.1 %fusion.13 = f32[4096,512]{1,0:T(8,128)} fusion(bf16[1024,512]{0,1:T(8,128)(2,1)S(1)} %bitcast.199, bf16[512,4096]{0,1:T(8,128)(2,1)S(1)} %bitcast.198, bf16[512,4096]{0,1:T(8,128)(2,1)} %bitcast.39), kind=kOutput, calls=%fused_computation.25 | convolution fusion | flops 4311744512 | bytes 17825792 | tf_op jit(solution)/shard_map/dot_general | solution.py:236
  230.4 5.1 %fusion.20 = f32[4,128,512,1]{2,1,3,0:T(8,128)} fusion(bf16[8,128,4,128]{3,2,1,0:T(4,128)(2,1)S(1)} %reshape.250, bf16[8,4,128,1024]{2,3,1,0:T(8,128)(2,1)} %fusion.70), kind=kOutput, calls=%fused_computation.37 | convolution fusion | flops 536870912 | bytes 6291456 | tf_op jit(solution)/shard_map/bhqk,bqhd->khd/dot_general | solution.py:285
  235.5 4.6 %fusion.82 = f32[8,4,128,512]{2,3,1,0:T(8,128)} fusion(bf16[8,128,4,128]{1,3,2,0:T(8,128)(2,1)S(1)} %copy.237, bf16[8,512,4,128]{1,3,2,0:T(8,128)(2,1)S(1)} %bitcast.179), kind=kOutput, calls=%fused_computation.169 | convolution fusion | flops 536870912 | bytes 13631488 | tf_op jit(solution)/shard_map/bqhd,bkhd->bhqk/dot_general | solution.py:246
  240.1 4.6 %convolution_bitcast_fusion = f32[8,4,128,512]{2,3,1,0:T(8,128)} fusion(bf16[512,4,128,1]{0,2,1,3:T(8,128)(2,1)S(1)} %bitcast.191, bf16[8,128,4,128]{1,3,2,0:T(8,128)(2,1)S(1)} %copy.237), kind=kOutput, calls=%fused_computation.55 | convolution fusion | flops 536870912 | bytes 9961472 | tf_op jit(solution)/shard_map/bqhd,khd->bhqk/dot_general | solution.py:249
  247.9 29.3 %multiply_convert_fusion = bf16[8,4,128,1024]{2,3,1,0:T(8,128)(2,1)} fusion(f32[8,4,128,512]{2,3,1,0:T(8,128)} %convolution_bitcast_fusion, f32[8,4,128,512]{2,3,1,0:T(8,128)} %fusion.82, f32[8,4,128,1024]{2,3,1,0:T(8,128)} %copy-done.12, f32[8,4,128]{2,1,0:T(4,128)S(1)} %get-tuple-element.94), kind=kOutput, calls=%fused_computation.13 | output fusion | flops 33559552 | bytes 41959424 | tf_op jit(solution)/shard_map/sub | solution.py:256
  277.2 4.6 %fusion.49 = f32[4,512,128]{1,2,0:T(8,128)} fusion(bf16[8,128,4,128]{1,3,2,0:T(8,128)(2,1)S(1)} %copy-done.9, bf16[8,4,128,1024]{2,3,1,0:T(8,128)(2,1)} %multiply_convert_fusion), kind=kOutput, calls=%fused_computation.84 | convolution fusion | flops 537133056 | bytes 6291456 | tf_op jit(solution)/shard_map/bhqk,bqhd->khd/dot_general | solution.py:282
  283.5 3.6 collective-permute-start.19
  287.0 3.8 fusion.30
  290.8 3.5 broadcast_multiply_fusion
  294.4 7.2 %fusion.16 = (f32[2,8,128,512]{2,3,1,0:T(8,128)}, f32[2,8,128,512]{2,3,1,0:T(8,128)}, f32[2,8,128,512]{2,3,1,0:T(8,128)}, f32[2,8,128,512]{2,3,1,0:T(8,128)}) fusion(f32[1,8,512,512]{2,3,1,0:T(8,128)S(1)} %bitcast.181, f32[1,8,512,512]{2,3,1,0:T(8,128)S(1)} %bitcast.180), kind=kLoop, calls=%fused_computation.28 | loop fusion | flops 4194304 | bytes 33554432 | tf_op jit(solution)/shard_map/stack | solution.py:280
  301.6 3.7 fusion.24
  305.3 4.2 fusion.39
  311.9 3.7 reduce_sum.103
  324.8 6.1 %collective-permute-done.20 = f32[2,128,512]{2,1,0:T(8,128)S(1)} collective-permute-done((f32[2,128,512]{2,1,0:T(8,128)S(1)}, f32[2,128,512]{2,1,0:T(8,128)S(1)}, u32[]{:S(2)}, u32[]{:S(2)}) %collective-permute-start.20) | collective-permute-done | bytes 524320 | tf_op jit(solution)/shard_map/ppermute | solution.py:23
  342.2 5.4 %copy.239 = f32[2,8,128,512]{3,2,1,0:T(8,128)} copy(f32[2,8,128,512]{2,3,1,0:T(8,128)} %get-tuple-element.49) | data formatting | bytes 8388608 | tf_op jit(solution)/shard_map/slice | solution.py:289
  350.4 4.1 reduce_sum.102
  357.1 3.1 fusion.73
  365.2 3.3 broadcast_in_dim.44
  368.5 3.6 reshape.263
  385.8 3.5 broadcast_in_dim.45
  389.3 6.5 %reshape.264 = f32[2,1024,512]{2,1,0:T(8,128)} reshape(f32[2,512,2,512]{3,2,1,0:T(2,128)} %broadcast_in_dim.45) | data formatting | bytes 8388608 | tf_op jit(solution)/shard_map/reshape | solution.py:37
  413.8 3.0 fusion.84
  418.1 3.9 add_convert_fusion
  (236 shorter events, 137.1 us)
Async XLA Ops:
  9.0 65.8 %collective-permute-start.9 = (bf16[512,512]{1,0:T(8,128)(2,1)}, bf16[512,512]{1,0:T(8,128)(2,1)}, u32[]{:S(2)}, u32[]{:S(2)}) collective-permute-start(bf16[512,512]{1,0:T(8,128)(2,1)} %slice.169), channel_id=1, source_target_pairs={{0,1},{1,0},{2,3},{3,2},{4,5},{5,4},{6,7},{7,6},{8,9},{9,8},{10,11... | collective-permute-start | bytes 1572872 | tf_op jit(solution)/shard_map/ppermute | solution.py:46
  10.7 10.3 %copy-start.3 = (bf16[1024,512]{1,0:T(8,128)(2,1)S(1)}, bf16[1024,512]{1,0:T(8,128)(2,1)}, u32[]{:S(2)}) copy-start(bf16[1024,512]{1,0:T(8,128)(2,1)} %param.7) | copy-start | bytes 3145732
  14.5 37.1 %collective-permute-start = (f32[2,128,512]{2,1,0:T(8,128)}, f32[2,128,512]{2,1,0:T(8,128)}, u32[]{:S(2)}, u32[]{:S(2)}) collective-permute-start(f32[2,128,512]{2,1,0:T(8,128)} %broadcast_multiply_fusion.3), channel_id=1, source_target_pairs={{0,8},{8,0},{16,24},{24,16},{32,40},{40,32},{48,56},{56,48},{64,72... | collective-permute-start | bytes 1572872 | tf_op jit(solution)/shard_map/ppermute | solution.py:23
  14.5 9.3 %copy-start.2 = (bf16[1024,512]{1,0:T(8,128)(2,1)S(1)}, bf16[1024,512]{1,0:T(8,128)(2,1)}, u32[]{:S(2)}) copy-start(bf16[1024,512]{1,0:T(8,128)(2,1)} %param.8) | copy-start | bytes 3145732
  17.8 71.6 %collective-permute-start.6 = (bf16[512,512]{1,0:T(8,128)(2,1)}, bf16[512,512]{1,0:T(8,128)(2,1)}, u32[]{:S(2)}, u32[]{:S(2)}) collective-permute-start(bf16[512,512]{1,0:T(8,128)(2,1)} %get-tuple-element.60), channel_id=1, source_target_pairs={{0,5},{1,6},{2,7},{3,0},{4,1},{5,2},{6,3},{7,4},{8,14},{9,15},{10,... | collective-permute-start | bytes 1572872 | tf_op jit(solution)/shard_map/ppermute | solution.py:98
  21.0 75.3 %collective-permute-start.5 = (bf16[512,512]{1,0:T(8,128)(2,1)}, bf16[512,512]{1,0:T(8,128)(2,1)}, u32[]{:S(2)}, u32[]{:S(2)}) collective-permute-start(bf16[512,512]{1,0:T(8,128)(2,1)} %get-tuple-element.61), channel_id=1, source_target_pairs={{0,3},{1,4},{2,5},{3,6},{4,7},{5,0},{6,1},{7,2},{8,12},{9,13},{10,... | collective-permute-start | bytes 1572872 | tf_op jit(solution)/shard_map/ppermute | solution.py:98
  29.0 108.3 %copy-start.8 = (bf16[8,128,4,128]{1,3,2,0:T(8,128)(2,1)}, bf16[8,128,4,128]{1,3,2,0:T(8,128)(2,1)S(1)}, u32[]{:S(2)}) copy-start(bf16[8,128,4,128]{1,3,2,0:T(8,128)(2,1)S(1)} %copy.218) | copy-start | bytes 3145732
  54.9 15.8 %collective-permute-start.1 = (f32[2,128,512]{2,1,0:T(8,128)S(1)}, f32[2,128,512]{2,1,0:T(8,128)S(1)}, u32[]{:S(2)}, u32[]{:S(2)}) collective-permute-start(f32[2,128,512]{2,1,0:T(8,128)S(1)} %copy_multiply_fusion.2), channel_id=1, source_target_pairs={{0,16},{8,24},{16,0},{24,8},{32,48},{40,56},{48,32},{56,40},{64,80... | collective-permute-start | bytes 1572872 | tf_op jit(solution)/shard_map/ppermute | solution.py:23
  62.6 12.2 %copy-start.32 = (bf16[1024,512]{1,0:T(8,128)(2,1)S(1)}, bf16[1024,512]{1,0:T(8,128)(2,1)}, u32[]{:S(2)}) copy-start(bf16[1024,512]{1,0:T(8,128)(2,1)} %param.10) | copy-start | bytes 3145732
  70.7 7.7 %copy-start.37 = (f32[2,128,512]{2,1,0:T(8,128)}, f32[2,128,512]{2,1,0:T(8,128)S(1)}, u32[]{:S(2)}) copy-start(f32[2,128,512]{2,1,0:T(8,128)S(1)} %collective-permute-done.1) | copy-start | bytes 1572868
  72.9 14.0 %collective-permute-start.2 = (f32[2,128,512]{2,1,0:T(8,128)}, f32[2,128,512]{2,1,0:T(8,128)}, u32[]{:S(2)}, u32[]{:S(2)}) collective-permute-start(f32[2,128,512]{2,1,0:T(8,128)} %copy_multiply_fusion.1), channel_id=1, source_target_pairs={{0,32},{8,40},{16,48},{24,56},{32,0},{40,8},{48,16},{56,24},{64,96... | collective-permute-start | bytes 1572872 | tf_op jit(solution)/shard_map/ppermute | solution.py:23
  78.4 49.4 %collective-permute-start.10 = (bf16[512,1024]{1,0:T(8,128)(2,1)}, bf16[512,1024]{1,0:T(8,128)(2,1)S(1)}, u32[]{:S(2)}, u32[]{:S(2)}) collective-permute-start(bf16[512,1024]{1,0:T(8,128)(2,1)} %get-tuple-element.87), channel_id=1, source_target_pairs={{0,6},{1,7},{2,0},{3,1},{4,2},{5,3},{6,4},{7,5},{8,14},{9,15},{10,... | collective-permute-start | bytes 3145736 | tf_op jit(solution)/shard_map/ppermute | solution.py:57
  79.5 52.3 %collective-permute-start.11 = (bf16[512,1024]{1,0:T(8,128)(2,1)}, bf16[512,1024]{1,0:T(8,128)(2,1)S(1)}, u32[]{:S(2)}, u32[]{:S(2)}) collective-permute-start(bf16[512,1024]{1,0:T(8,128)(2,1)} %get-tuple-element.87), channel_id=1, source_target_pairs={{0,2},{1,3},{2,4},{3,5},{4,6},{5,7},{6,0},{7,1},{8,10},{9,11},{10,... | collective-permute-start | bytes 3145736 | tf_op jit(solution)/shard_map/ppermute | solution.py:56
  87.0 15.0 %collective-permute-start.4 = (bf16[512,512]{1,0:T(8,128)(2,1)}, bf16[512,512]{1,0:T(8,128)(2,1)}, u32[]{:S(2)}, u32[]{:S(2)}) collective-permute-start(bf16[512,512]{1,0:T(8,128)(2,1)} %get-tuple-element.62), channel_id=1, source_target_pairs={{0,1},{1,2},{2,3},{3,4},{4,5},{5,6},{6,7},{7,0},{8,10},{9,11},{10,... | collective-permute-start | bytes 1572872 | tf_op jit(solution)/shard_map/ppermute | solution.py:98
  89.4 13.2 %collective-permute-start.7 = (bf16[512,512]{1,0:T(8,128)(2,1)}, bf16[512,512]{1,0:T(8,128)(2,1)}, u32[]{:S(2)}, u32[]{:S(2)}) collective-permute-start(bf16[512,512]{1,0:T(8,128)(2,1)} %get-tuple-element.63), channel_id=1, source_target_pairs={{0,7},{1,0},{2,1},{3,2},{4,3},{5,4},{6,5},{7,6},{16,23},{17,16},{1... | collective-permute-start | bytes 1572872 | tf_op jit(solution)/shard_map/ppermute | solution.py:98
  96.2 37.7 %collective-permute-start.3 = (bf16[2,128,512]{2,1,0:T(8,128)(2,1)S(1)}, bf16[2,128,512]{2,1,0:T(8,128)(2,1)}, u32[]{:S(2)}, u32[]{:S(2)}) collective-permute-start(bf16[2,128,512]{2,1,0:T(8,128)(2,1)S(1)} %copy_multiply_fusion), channel_id=1, source_target_pairs={{0,64},{8,72},{16,80},{24,88},{32,96},{40,104},{48,112},{56,120},{... | collective-permute-start | bytes 786440 | tf_op jit(solution)/shard_map/ppermute | solution.py:23
  102.0 16.7 %copy-start.38 = (bf16[512,512]{0,1:T(8,128)(2,1)S(1)}, bf16[512,512]{0,1:T(8,128)(2,1)}, u32[]{:S(2)}) copy-start(bf16[512,512]{0,1:T(8,128)(2,1)} %copy.210) | copy-start | bytes 1572868
  105.7 94.9 %collective-permute-start.8 = (bf16[4,512,512]{2,1,0:T(8,128)(2,1)}, bf16[4,512,512]{2,1,0:T(8,128)(2,1)}, u32[]{:S(2)}, u32[]{:S(2)}) collective-permute-start(bf16[4,512,512]{2,1,0:T(8,128)(2,1)} %pad_maximum_fusion.10), channel_id=1, source_target_pairs={{0,8},{8,0},{16,24},{24,16},{32,40},{40,32},{48,56},{56,48},{64,72... | collective-permute-start | bytes 6291464 | tf_op jit(solution)/shard_map/ppermute | solution.py:100
  121.0 86.8 %all-to-all-start = ((bf16[8,512,512]{1,2,0:T(8,128)(2,1)}), bf16[8,512,512]{1,2,0:T(8,128)(2,1)}, u32[]{:S(2)}, u32[]{:S(2)}) async-start(bf16[8,512,512]{1,2,0:T(8,128)(2,1)} %stack.112), calls=%async_computation | async-start | bytes 8388608 | tf_op jit(solution)/shard_map/all_to_all | solution.py:15
  125.6 296.4 %reduce-scatter.2.cloned.1.call-start = ((), (), s32[]{:S(2)}) async-start(), calls=%async_computation.2 | async-start | bytes 8912896 | tf_op jit(solution)/shard_map/reduce_scatter | solution.py:235
  127.8 8.3 %copy-start.33 = (bf16[512,1024]{1,0:T(8,128)(2,1)}, bf16[512,1024]{1,0:T(8,128)(2,1)S(1)}, u32[]{:S(2)}) copy-start(bf16[512,1024]{1,0:T(8,128)(2,1)S(1)} %collective-permute-done.10) | copy-start | bytes 3145732
  128.7 55.9 %collective-permute-start.13 = (bf16[512,512]{1,0:T(8,128)(2,1)}, bf16[512,512]{1,0:T(8,128)(2,1)}, u32[]{:S(2)}, u32[]{:S(2)}) collective-permute-start(bf16[512,512]{1,0:T(8,128)(2,1)} %slice.220), channel_id=1, source_target_pairs={{0,6},{1,7},{2,0},{3,1},{4,2},{5,3},{6,4},{7,5},{8,14},{9,15},{10,... | collective-permute-start | bytes 1572872 | tf_op jit(solution)/shard_map/ppermute | solution.py:63
  132.7 53.1 %collective-permute-start.12 = (bf16[512,512]{1,0:T(8,128)(2,1)}, bf16[512,512]{1,0:T(8,128)(2,1)}, u32[]{:S(2)}, u32[]{:S(2)}) collective-permute-start(bf16[512,512]{1,0:T(8,128)(2,1)} %slice.219), channel_id=1, source_target_pairs={{0,2},{1,3},{2,4},{3,5},{4,6},{5,7},{6,0},{7,1},{8,10},{9,11},{10,... | collective-permute-start | bytes 1572872 | tf_op jit(solution)/shard_map/ppermute | solution.py:62
  146.5 8.3 %copy-start.12 = (f32[8,4,128,1024]{2,3,1,0:T(8,128)}, f32[8,4,128,1024]{2,3,1,0:T(8,128)S(1)}, u32[]{:S(2)}) copy-start(f32[8,4,128,1024]{2,3,1,0:T(8,128)S(1)} %get-tuple-element.95) | copy-start | bytes 50331652
  146.5 8.3 %copy-start.40 = (bf16[1,512,512]{2,1,0:T(8,128)(2,1)S(1)}, bf16[1,512,512]{2,1,0:T(8,128)(2,1)}, u32[]{:S(2)}) copy-start(bf16[1,512,512]{2,1,0:T(8,128)(2,1)} %get-tuple-element.91) | copy-start | bytes 1572868
  161.9 25.1 %copy-start.31 = (bf16[1,512,1024]{2,1,0:T(8,128)(2,1)S(1)}, bf16[1,512,1024]{2,1,0:T(8,128)(2,1)}, u32[]{:S(2)}) copy-start(bf16[1,512,1024]{2,1,0:T(8,128)(2,1)} %get-tuple-element.86) | copy-start | bytes 3145732
  161.9 25.1 %copy-start.34 = (bf16[512,1024]{1,0:T(8,128)(2,1)S(1)}, bf16[512,1024]{1,0:T(8,128)(2,1)}, u32[]{:S(2)}) copy-start(bf16[512,1024]{1,0:T(8,128)(2,1)} %copy-done.33) | copy-start | bytes 3145732
  161.9 25.1 %copy-start.36 = (bf16[512,1024]{1,0:T(8,128)(2,1)S(1)}, bf16[512,1024]{1,0:T(8,128)(2,1)}, u32[]{:S(2)}) copy-start(bf16[512,1024]{1,0:T(8,128)(2,1)} %copy-done.35) | copy-start | bytes 3145732
  162.9 55.2 %copy-start.26 = (bf16[64,8,8,128]{3,1,2,0:T(8,128)(2,1)}, bf16[64,8,8,128]{3,1,2,0:T(8,128)(2,1)S(1)}, u32[]{:S(2)}) copy-start(bf16[64,8,8,128]{3,1,2,0:T(8,128)(2,1)S(1)} %copy.302) | copy-start | bytes 3145732
  207.8 10.3 %copy-start.25 = (bf16[512,4,1024]{0,2,1:T(8,128)(2,1)S(1)}, bf16[512,4,1024]{0,2,1:T(8,128)(2,1)}, u32[]{:S(2)}) copy-start(bf16[512,4,1024]{0,2,1:T(8,128)(2,1)} %copy.211) | copy-start | bytes 12582916
  230.4 14.3 %copy-start.11 = (bf16[8,128,4,128]{1,3,2,0:T(8,128)(2,1)}, bf16[8,128,4,128]{1,3,2,0:T(8,128)(2,1)S(1)}, u32[]{:S(2)}) copy-start(bf16[8,128,4,128]{1,3,2,0:T(8,128)(2,1)S(1)} %copy.237) | copy-start | bytes 3145732
  246.3 30.8 %copy-start.9 = (bf16[8,128,4,128]{1,3,2,0:T(8,128)(2,1)S(1)}, bf16[8,128,4,128]{1,3,2,0:T(8,128)(2,1)}, u32[]{:S(2)}) copy-start(bf16[8,128,4,128]{1,3,2,0:T(8,128)(2,1)} %copy-done.8) | copy-start | bytes 3145732
  246.3 72.9 %collective-permute-start.14 = (bf16[1024,512]{0,1:T(8,128)(2,1)}, bf16[1024,512]{0,1:T(8,128)(2,1)}, u32[]{:S(2)}, u32[]{:S(2)}) collective-permute-start(bf16[1024,512]{0,1:T(8,128)(2,1)} %bitcast.200), channel_id=1, source_target_pairs={{0,1},{1,0},{2,3},{3,2},{4,5},{5,4},{6,7},{7,6},{8,9},{9,8},{10,11... | collective-permute-start | bytes 3145736 | tf_op jit(solution)/shard_map/ppermute | solution.py:46
  283.4 7.4 %copy-start.6 = (f32[1,512,512]{2,1,0:T(8,128)}, f32[1,512,512]{2,1,0:T(8,128)S(1)}, u32[]{:S(2)}) copy-start(f32[1,512,512]{2,1,0:T(8,128)S(1)} %copy.221) | copy-start | bytes 3145732
  283.4 7.4 %copy-start.10 = (bf16[8,128,4,128]{1,3,2,0:T(8,128)(2,1)S(1)}, bf16[8,128,4,128]{1,3,2,0:T(8,128)(2,1)}, u32[]{:S(2)}) copy-start(bf16[8,128,4,128]{1,3,2,0:T(8,128)(2,1)} %copy-done.8) | copy-start | bytes 3145732
  283.5 32.1 %collective-permute-start.19 = (f32[2,128,512]{2,1,0:T(8,128)S(1)}, f32[2,128,512]{2,1,0:T(8,128)}, u32[]{:S(2)}, u32[]{:S(2)}) collective-permute-start(f32[2,128,512]{2,1,0:T(8,128)S(1)} %fusion.56), channel_id=1, source_target_pairs={{0,64},{8,72},{16,80},{24,88},{32,96},{40,104},{48,112},{56,120},{... | collective-permute-start | bytes 1572872 | tf_op jit(solution)/shard_map/ppermute | solution.py:23
  294.4 7.3 %copy-start.1 = (bf16[1,8,512,512]{2,3,1,0:T(8,128)(2,1)S(1)}, bf16[1,8,512,512]{2,3,1,0:T(8,128)(2,1)}, u32[]{:S(2)}) copy-start(bf16[1,8,512,512]{2,3,1,0:T(8,128)(2,1)} %copy.194) | copy-start | bytes 12582916
  317.8 6.9 %copy-start.28 = (f32[2,2,128,512]{2,3,1,0:T(8,128)S(1)}, f32[2,2,128,512]{2,3,1,0:T(8,128)}, u32[]{:S(2)}) copy-start(f32[2,2,128,512]{2,3,1,0:T(8,128)} %reduce_sum.103) | copy-start | bytes 3145732
  318.1 12.9 %collective-permute-start.20 = (f32[2,128,512]{2,1,0:T(8,128)S(1)}, f32[2,128,512]{2,1,0:T(8,128)S(1)}, u32[]{:S(2)}, u32[]{:S(2)}) collective-permute-start(f32[2,128,512]{2,1,0:T(8,128)S(1)} %fusion.58), channel_id=1, source_target_pairs={{0,32},{8,40},{16,48},{24,56},{32,0},{40,8},{48,16},{56,24},{64,96... | collective-permute-start | bytes 1572872 | tf_op jit(solution)/shard_map/ppermute | solution.py:23
  321.5 54.7 %collective-permute-start.16 = (bf16[1024,1024]{0,1:T(8,128)(2,1)}, bf16[1024,1024]{0,1:T(8,128)(2,1)}, u32[]{:S(2)}, u32[]{:S(2)}) collective-permute-start(bf16[1024,1024]{0,1:T(8,128)(2,1)} %constant_dynamic-update-slice_fusion), channel_id=1, source_target_pairs={{0,2},{1,3},{2,4},{3,5},{4,6},{5,7},{6,0},{7,1},{8,10},{9,11},{10,... | collective-permute-start | bytes 6291464 | tf_op jit(solution)/shard_map/ppermute | solution.py:56
  322.0 57.7 %collective-permute-start.15 = (bf16[1024,1024]{0,1:T(8,128)(2,1)}, bf16[1024,1024]{0,1:T(8,128)(2,1)}, u32[]{:S(2)}, u32[]{:S(2)}) collective-permute-start(bf16[1024,1024]{0,1:T(8,128)(2,1)} %constant_dynamic-update-slice_fusion), channel_id=1, source_target_pairs={{0,6},{1,7},{2,0},{3,1},{4,2},{5,3},{6,4},{7,5},{8,14},{9,15},{10,... | collective-permute-start | bytes 6291464 | tf_op jit(solution)/shard_map/ppermute | solution.py:57
  333.3 40.5 %collective-permute-start.21 = (f32[2,128,512]{2,1,0:T(8,128)}, f32[2,128,512]{2,1,0:T(8,128)}, u32[]{:S(2)}, u32[]{:S(2)}) collective-permute-start(f32[2,128,512]{2,1,0:T(8,128)} %fusion.55), channel_id=1, source_target_pairs={{0,16},{8,24},{16,0},{24,8},{32,48},{40,56},{48,32},{56,40},{64,80... | collective-permute-start | bytes 1572872 | tf_op jit(solution)/shard_map/ppermute | solution.py:23
  376.2 9.5 %copy-start.18 = (f32[2,128,512]{2,0,1:T(2,128)}, f32[2,128,512]{2,0,1:T(2,128)S(1)}, u32[]{:S(2)}) copy-start(f32[2,128,512]{2,0,1:T(2,128)S(1)} %get-tuple-element.80) | copy-start | bytes 1572868
  376.2 9.0 %copy-start.16 = (f32[2,512,512]{2,1,0:T(8,128)S(1)}, f32[2,512,512]{2,1,0:T(8,128)}, u32[]{:S(2)}) copy-start(f32[2,512,512]{2,1,0:T(8,128)} %reshape.263) | copy-start | bytes 6291460
  378.7 24.5 %collective-permute-start.17 = (bf16[1024,512]{0,1:T(8,128)(2,1)}, bf16[1024,512]{0,1:T(8,128)(2,1)}, u32[]{:S(2)}, u32[]{:S(2)}) collective-permute-start(bf16[1024,512]{0,1:T(8,128)(2,1)} %slice.221), channel_id=1, source_target_pairs={{0,2},{1,3},{2,4},{3,5},{4,6},{5,7},{6,0},{7,1},{8,10},{9,11},{10,... | collective-permute-start | bytes 3145736 | tf_op jit(solution)/shard_map/ppermute | solution.py:62
  382.0 23.6 %collective-permute-start.18 = (bf16[1024,512]{0,1:T(8,128)(2,1)}, bf16[1024,512]{0,1:T(8,128)(2,1)}, u32[]{:S(2)}, u32[]{:S(2)}) collective-permute-start(bf16[1024,512]{0,1:T(8,128)(2,1)} %slice.222), channel_id=1, source_target_pairs={{0,6},{1,7},{2,0},{3,1},{4,2},{5,3},{6,4},{7,5},{8,14},{9,15},{10,... | collective-permute-start | bytes 3145736 | tf_op jit(solution)/shard_map/ppermute | solution.py:63
  385.3 15.3 %collective-permute-start.22 = (f32[2,128,512]{2,1,0:T(8,128)}, f32[2,128,512]{2,1,0:T(8,128)S(1)}, u32[]{:S(2)}, u32[]{:S(2)}) collective-permute-start(f32[2,128,512]{2,1,0:T(8,128)} %fusion.59), channel_id=1, source_target_pairs={{0,8},{8,0},{16,24},{24,16},{32,40},{40,32},{48,56},{56,48},{64,72... | collective-permute-start | bytes 1572872 | tf_op jit(solution)/shard_map/ppermute | solution.py:23
  397.6 9.7 %copy-start.14 = (f32[2,1024,512]{2,1,0:T(8,128)S(1)}, f32[2,1024,512]{2,1,0:T(8,128)}, u32[]{:S(2)}) copy-start(f32[2,1024,512]{2,1,0:T(8,128)} %reshape.264) | copy-start | bytes 12582916
  (24 other events, 88.8 us)
Sparse Core Ops, SparseCore 0:
  244.9 114.4 reduce-scatter.1
